TPU v7x, 128 devices: a whole 4x4x4 slice. The times are simulated.
128 devices in a mesh: leaf: 16 (over z, y), col: 8 (over x, core).
Axes of the slice: x: 4, y: 4, z: 4, core: 2. Of those that a mesh axis runs over, the one named last changes fastest.
Arguments:
- child_fronts: float32 [16, 4096, 4096], P('leaf', 'col'), may hold values from -8 to 8, as said below
- child_index: int32 [16, 14], replicated, may hold values from 0 to 47, as said below
- parent_front: float32 [12288, 12288], P('leaf', 'col'), may hold values from -8 to 8, as said below
Outputs:
- child_factor: float32 [16, 4096, 512], P('leaf', 'col')
- parent_factor: float32 [12288, 12288], P('leaf', 'col')
Inputs may be any that keep to these rules, and one draw needn't show every extreme that they name: `child_index`: in each row the 14 indices are distinct and so are their groups index // 3; hence one row names at most 2 indices in any aligned group of 6 blocks (blocks 6k to 6k+5), and exactly 2 in some. `child_fronts`: each child front is symmetric with diagonal entries of 0.5 to 7 and smallest eigenvalue above 0.5. `parent_front`: symmetric with diagonal entries of 0.5 to 7 and smallest eigenvalue above 0.5.
All inputs are finite; a program needn't handle non-finite values.
Results may differ from a plain program's by a relative error of at most 0.00016.
Values sent between devices are 32-bit elements; how exact they have to be, the bound alone decides.
No kernel may reach another device: no remote copies, remote signals or barrier semaphores. Data moves between devices by JAX's collectives and lax.ppermute only.
A program may use at most 192 MiB of HBM per device.

v0:
```python
import jax
import jax.numpy as jnp
from jax import lax
from jax.sharding import PartitionSpec as P

B = 256
PC = 2
ROWBLK = 3


highest = lax.Precision.HIGHEST


def spread_2(shard, axis, root):
    mine = lax.axis_index(axis) == root
    return lax.psum(jnp.where(mine, shard, jnp.zeros_like(shard)), axis)


def solve_rows(factor, rows):
    return jax.scipy.linalg.solve_triangular(factor, rows.T, lower=True).T


def route_slots(indices, col_blocks):
    target = indices // col_blocks
    count = indices.shape[-1]
    earlier_mask = lax.broadcasted_iota(jnp.int32, (count, count), 1) < lax.broadcasted_iota(
        jnp.int32, (count, count), 0
    )
    same = target[..., :, None] == target[..., None, :]
    ranking = jnp.sum((same & earlier_mask).astype(jnp.int32), axis=-1)
    return (target, ranking)


def per_device(child_fronts, child_index, parent_front):
    leaf_pos = lax.axis_index("leaf")
    col_pos = lax.axis_index("col")
    leaf_count = lax.axis_size("leaf")
    col_count = lax.axis_size("col")
    share = leaf_count // col_count
    children = child_index.shape[0]
    contrib_count = child_index.shape[1]
    front_rows = child_fronts[0]
    row_count = front_rows.shape[0]
    pivot_width = PC * B
    raw_panel = front_rows[:, :pivot_width]
    whole_panel = lax.all_gather(raw_panel, "col", axis=0, tiled=True)
    pivot_factor = jnp.linalg.cholesky(whole_panel[:pivot_width])
    solved_all = solve_rows(pivot_factor, whole_panel)
    own_rows = lax.dynamic_slice_in_dim(solved_all, col_pos * row_count, row_count, 0)
    first_device = col_pos == 0
    child_out = jnp.where(first_device, pivot_factor, own_rows)[None]
    update_rows = front_rows[:, pivot_width:] - jnp.dot(
        own_rows, solved_all[pivot_width:].T, precision=highest, preferred_element_type=jnp.float32
    )
    update_rows = jnp.where(first_device, 0.0, update_rows)
    col_blocks = ROWBLK * leaf_count // col_count
    own_index = lax.dynamic_index_in_dim(child_index, leaf_pos, 0, keepdims=False)
    target, ranking = route_slots(own_index, col_blocks)
    slot_ids = jnp.arange(col_count * share, dtype=jnp.int32)
    selector = (slot_ids[:, None] == (target * share + ranking)[None, :]).astype(jnp.float32)
    selector = selector.reshape(col_count, share, contrib_count)
    pieces = update_rows.reshape(row_count, contrib_count, B)
    outgoing = jnp.einsum("msc,rcb->mrsb", selector, pieces, precision=highest)
    incoming = lax.all_to_all(outgoing, "col", split_axis=0, concat_axis=0, tiled=True)
    columns = incoming.reshape(col_count * row_count, share * B)
    contrib_rows = columns[pivot_width:].reshape(contrib_count, B, share * B)
    leaf_target = own_index // ROWBLK
    row_select = (jnp.arange(leaf_count, dtype=jnp.int32)[:, None] == leaf_target[None, :]).astype(
        jnp.float32
    )
    outgoing_rows = jnp.einsum("lr,rbx->lbx", row_select, contrib_rows, precision=highest)
    arrived = lax.all_to_all(outgoing_rows, "leaf", split_axis=0, concat_axis=0, tiled=True)
    all_target, all_rank = route_slots(child_index, col_blocks)
    local_col = child_index - col_pos * col_blocks
    hits = (all_target == col_pos)[:, :, None, None]
    hits = hits & (
        all_rank[:, :, None, None] == jnp.arange(share, dtype=jnp.int32)[None, None, :, None]
    )
    hits = hits & (
        local_col[:, :, None, None] == jnp.arange(col_blocks, dtype=jnp.int32)[None, None, None, :]
    )
    col_select = jnp.sum(hits.astype(jnp.float32), axis=1)
    local_row = child_index - leaf_pos * ROWBLK
    row_place = jnp.sum(
        (local_row[:, :, None] == jnp.arange(ROWBLK, dtype=jnp.int32)[None, None, :]).astype(
            jnp.float32
        ),
        axis=1,
    )
    arrived_blocks = arrived.reshape(children, B, share, B)
    spread = jnp.einsum("gsq,gbse->gbqe", col_select, arrived_blocks, precision=highest)
    update = jnp.einsum("gp,gbqe->pbqe", row_place, spread, precision=highest)
    assembled = parent_front + update.reshape(ROWBLK * B, col_blocks * B)
    parent_pivots = ROWBLK * B
    raw_rows = spread_2(assembled[:, :parent_pivots], "col", 0)
    received = []
    for turn in range(share + 1):
        root = col_pos * 0 if turn == 0 else col_pos * share + turn - 1
        received.append(spread_2(raw_rows, "leaf", root))
    parent_pivot = jnp.linalg.cholesky(received[0])
    row_panel = solve_rows(parent_pivot, raw_rows)
    col_panel = solve_rows(parent_pivot, jnp.concatenate(received[1:], 0))
    schur = assembled - jnp.dot(
        row_panel, col_panel.T, precision=highest, preferred_element_type=jnp.float32
    )
    left = jnp.where(leaf_pos == 0, parent_pivot, row_panel)
    left_full = jnp.concatenate(
        [left, jnp.zeros((left.shape[0], assembled.shape[1] - parent_pivots), jnp.float32)], 1
    )
    global_row = leaf_pos * assembled.shape[0] + lax.broadcasted_iota(jnp.int32, assembled.shape, 0)
    global_col = col_pos * assembled.shape[1] + lax.broadcasted_iota(jnp.int32, assembled.shape, 1)
    parent_out = jnp.where(
        global_col < parent_pivots, left_full, jnp.where(global_row < parent_pivots, 0.0, schur)
    )
    return (child_out, parent_out)


def solution(mesh):
    placed = (P("leaf", "col", None), P(), P("leaf", "col"))
    return jax.shard_map(
        per_device,
        mesh=mesh,
        in_specs=placed,
        out_specs=(P("leaf", "col", None), P("leaf", "col")),
        check_vma=False,
    )
```

profile of v0, /device:TPU:1, one launch (start us, length us, event | category | flops | bytes accessed | tf_op | source)
XLA Modules:
  0.0 1161.2 jit_solution(11400837171612983125)
XLA Ops:
  7.2 9.0 copy.88
  18.8 53.1 %all-gather.2.cloned.1.call-done = f32[4096,512]{0,1:T(8,128)} async-done(((f32[512,512]{0,1:T(8,128)}), f32[4096,512]{0,1:T(8,128)}) %all-gather.2.cloned.1.call-update) | async-done | bytes 8388624 | tf_op jit(solution)/shard_map/all_gather | solution.py:46
  74.9 11.7 %cholesky.221 = f32[128,128]{1,0:T(8,128)S(1)} custom-call(f32[128,128]{1,0:T(8,128)S(1)} %cholesky.570), custom_call_target="Cholesky" | custom-call | tf_op jit(solution)/shard_map/jit(cholesky)/cholesky | solution.py:47
  86.8 9.8 custom-call.67
  97.3 11.7 %cholesky.235 = f32[128,128]{1,0:T(8,128)S(1)} custom-call(f32[128,128]{1,0:T(8,128)S(1)} %cholesky.574), custom_call_target="Cholesky" | custom-call | tf_op jit(solution)/shard_map/jit(cholesky)/cholesky | solution.py:47
  109.1 10.0 custom-call.68
  119.8 11.7 %cholesky.254 = f32[128,128]{1,0:T(8,128)S(1)} custom-call(f32[128,128]{1,0:T(8,128)S(1)} %cholesky.579), custom_call_target="Cholesky" | custom-call | tf_op jit(solution)/shard_map/jit(cholesky)/cholesky | solution.py:47
  131.5 9.8 custom-call.69
  141.9 11.7 %cholesky.462 = f32[128,128]{1,0:T(8,128)S(1)} custom-call(f32[128,128]{1,0:T(8,128)S(1)} %convolution_subtract_fusion.17), custom_call_target="Cholesky" | custom-call | tf_op jit(solution)/shard_map/jit(cholesky)/cholesky | solution.py:47
  154.4 10.9 compare_reduce_fusion.6
  168.7 10.9 while.2
  179.7 40.2 %custom-call.60 = f32[4,128,128]{1,2,0:T(8,128)S(1)} custom-call(f32[4,128,128]{2,1,0:T(8,128)} %get-tuple-element.12), custom_call_target="InvertDiagBlocksLowerTriangular" | custom-call | tf_op jit(solution)/shard_map/jit(_solve_triangular)/triangular_solve | solution.py:20
  219.8 3.5 fusion.39
  223.3 3.6 convolution_subtract_fusion.1
  228.9 4.9 convolution_subtract_fusion
  237.1 6.4 fusion.15
  243.5 3.0 copy.95
  246.4 2.9 copy.94
  251.1 5.2 fusion.106
  256.4 3.5 fusion.155
  260.4 14.7 %fusion.6 = f32[512,3584]{0,1:T(8,128)} fusion(f32[512,4096]{0,1:T(8,128)S(1)} %bitcast.229, f32[4096,512]{1,0:T(8,128)S(1)} %get-tuple-element.73, pred[]{:T(512)S(6)} %eq.138, f32[512,4096]{0,1:T(8,128)S(1)} %get-tuple-element.74, s32[]{:T(128)S(6)} %select_n.93), kind=kOutput, calls=%fused_computation.13 | convolution fusion | flops 11277959168 | bytes 23068676 | tf_op jit(solution)/shard_map/dot_general | solution.py:52
  275.2 10.1 copy.127
  285.3 6.7 convolution_bitcast_fusion.1
  291.9 6.9 copy.99
  298.9 5.3 all-to-all-start
  304.2 93.7 %all-to-all-done = f32[8,512,2,256]{3,2,1,0:T(2,128)} async-done(((f32[8,512,2,256]{3,2,1,0:T(2,128)}), f32[8,512,2,256]{3,2,1,0:T(2,128)}, u32[]{:S(2)}, u32[]{:S(2)}) %all-to-all-start) | async-done | bytes 8388640 | tf_op jit(solution)/shard_map/all_to_all | solution.py:64
  397.9 8.6 slice.348
  406.5 10.5 reshape.199
  416.9 17.9 %fusion.2 = f32[16,256,512]{2,0,1:T(8,128)S(1)} fusion(f32[14,256,512]{2,1,0:T(8,128)} %reshape.199, s32[14]{0:T(128)S(1)} %fusion.145), kind=kOutput, calls=%fused_computation.8 | convolution fusion | flops 352321760 | bytes 15728696 | tf_op jit(solution)/shard_map/lr,rbx->lbx/dot_general | solution.py:71
  434.8 8.1 copy.101
  442.9 6.8 all-to-all-start.1
  449.7 6.5 copy.108
  457.2 114.9 %all-to-all-done.1 = f32[16,256,512]{2,1,0:T(8,128)} async-done(((f32[16,256,512]{2,1,0:T(8,128)}), f32[16,256,512]{2,1,0:T(8,128)}, u32[]{:S(2)}, u32[]{:S(2)}) %all-to-all-start.1) | async-done | bytes 8388640 | tf_op jit(solution)/shard_map/all_to_all | solution.py:72
  572.1 10.5 reshape.200
  582.6 34.3 %convolution_bitcast_fusion = f32[16,256,6,256]{3,2,1,0:T(8,128)} fusion(f32[16,256,2,256]{3,2,1,0:T(2,128)} %reshape.200, f32[16,2,6,1]{2,1,3,0:T(2,128)S(1)} %copy.128), kind=kOutput, calls=%fused_computation.6 | convolution fusion | flops 150994944 | bytes 33555200 | tf_op jit(solution)/shard_map/gsq,gbse->gbqe/dot_general | solution.py:91
  616.9 37.0 %fusion = f32[3,256,6,256]{3,0,2,1:T(4,128)} fusion(f32[16,256,6,256]{3,2,1,0:T(8,128)} %convolution_bitcast_fusion, f32[16,3]{0,1:T(4,128)S(1)} %convert_reduce_fusion.1), kind=kOutput, calls=%fused_computation.4 | convolution fusion | flops 226492416 | bytes 29884608 | tf_op jit(solution)/shard_map/gp,gbqe->pbqe/dot_general | solution.py:92
  653.9 8.8 copy.136
  662.7 3.9 copy.139
  666.6 3.0 add.148
  673.4 64.6 %all-reduce.7.cloned.1.call-done = f32[768,768]{0,1:T(8,128)} async-done(((f32[768,768]{0,1:T(8,128)}), f32[768,768]{0,1:T(8,128)}) %all-reduce.7.cloned.1.call-update) | async-done | bytes 2359312 | tf_op jit(solution)/shard_map/psum | solution.py:16
  738.0 4.6 broadcast_select_fusion.1
  742.7 2.4 fusion.65
  745.1 128.6 %all-reduce.9.cloned.1.call-done = (f32[768,768]{0,1:T(8,128)}, f32[768,768]{0,1:T(8,128)}, f32[768,768]{0,1:T(8,128)}) async-done(((f32[768,768]{0,1:T(8,128)}, f32[768,768]{0,1:T(8,128)}, f32[768,768]{0,1:T(8,128)}), (f32[768,768]{0,1:T(8,128)}, f32[768,768]{0,1:T(8,128)}, f32[768,768]{0,1:T(8,128)})) %all-reduce.9.cloned.1.call-update) | async-done | bytes 7077904 | tf_op jit(solution)/shard_map/psum | solution.py:16
  873.7 3.6 copy.110
  880.7 11.7 %cholesky.474 = f32[128,128]{1,0:T(8,128)S(1)} custom-call(f32[128,128]{1,0:T(8,128)S(1)} %cholesky.583), custom_call_target="Cholesky" | custom-call | tf_op jit(solution)/shard_map/jit(cholesky)/cholesky | solution.py:100
  892.6 9.8 custom-call.61
  905.4 11.7 %cholesky.492 = f32[128,128]{1,0:T(8,128)S(1)} custom-call(f32[128,128]{1,0:T(8,128)S(1)} %cholesky.587), custom_call_target="Cholesky" | custom-call | tf_op jit(solution)/shard_map/jit(cholesky)/cholesky | solution.py:100
  917.4 10.0 custom-call.62
  929.8 11.7 %cholesky.513 = f32[128,128]{1,0:T(8,128)S(1)} custom-call(f32[128,128]{1,0:T(8,128)S(1)} %cholesky.592), custom_call_target="Cholesky" | custom-call | tf_op jit(solution)/shard_map/jit(cholesky)/cholesky | solution.py:100
  941.7 9.8 custom-call.70
  954.0 12.1 %cholesky.528 = f32[128,128]{1,0:T(8,128)S(1)} custom-call(f32[128,128]{1,0:T(8,128)S(1)} %cholesky.597), custom_call_target="Cholesky" | custom-call | tf_op jit(solution)/shard_map/jit(cholesky)/cholesky | solution.py:100
  966.2 9.8 custom-call.71
  978.3 11.7 %cholesky.543 = f32[128,128]{1,0:T(8,128)S(1)} custom-call(f32[128,128]{1,0:T(8,128)S(1)} %cholesky.602), custom_call_target="Cholesky" | custom-call | tf_op jit(solution)/shard_map/jit(cholesky)/cholesky | solution.py:100
  990.1 9.8 custom-call.72
  1001.9 11.7 %cholesky.557 = f32[128,128]{1,0:T(8,128)S(1)} custom-call(f32[128,128]{1,0:T(8,128)S(1)} %convolution_subtract_fusion.16), custom_call_target="Cholesky" | custom-call | tf_op jit(solution)/shard_map/jit(cholesky)/cholesky | solution.py:100
  1023.4 22.1 %while.3 = (s32[]{:T(128)}, f32[768,768]{0,1:T(8,128)}, s32[6,2]{0,1:T(2,128)S(1)}, f32[6,128,128]{2,1,0:T(8,128)}, s32[]{:T(128)}) while((s32[]{:T(128)}, f32[768,768]{0,1:T(8,128)}, s32[6,2]{0,1:T(2,128)S(1)}, f32[6,128,128]{2,1,0:T(8,128)}, s32[]{:T(128)}) %tuple.89), condition=%wide.while_cond.1, body=%wide.while_body.1.sunk | while | flops 2 | bytes 393329 | solution.py:20
  1024.1 2.3 dynamic-slice.23
  1027.8 2.3 dynamic-slice.23
  1031.5 2.3 dynamic-slice.23
  1035.1 2.3 dynamic-slice.23
  1045.5 59.8 %custom-call.63 = f32[6,128,128]{1,2,0:T(8,128)S(1)} custom-call(f32[6,128,128]{2,1,0:T(8,128)} %get-tuple-element.20), custom_call_target="InvertDiagBlocksLowerTriangular" | custom-call | tf_op jit(solution)/shard_map/jit(_solve_triangular)/triangular_solve | solution.py:20
  1129.3 2.4 convolution_subtract_fusion.3
  1132.6 15.6 %select_select_fusion = f32[768,1536]{0,1:T(8,128)} fusion(f32[768,1536]{0,1:T(8,128)S(1)} %bitcast.231, f32[768,768]{0,1:T(8,128)S(1)} %bitcast_select_fusion, f32[768,768]{1,0:T(8,128)S(1)} %convolution_dynamic-update-slice_fusion.1, f32[768,1536]{1,0:T(8,128)S(1)} %convolution_dynamic-update-slice_fusion, pred[1536]{0:T(1024)(128)(4,1)S(1)} %add_compare_fusion, ...), kind=kOutput, calls=%fused_computation.24 | convolution fusion | flops 10875174912 | bytes 18876672 | tf_op jit(solution)/shard_map/dot_general | solution.py:103
  1148.2 6.0 copy.121
  (201 shorter events, 92.2 us)
Async XLA Ops:
  7.2 64.7 %all-gather.2.cloned.1.call-start = ((), (), s32[]{:S(2)}) async-start(), calls=%async_computation.2 | async-start | bytes 9437184 | tf_op jit(solution)/shard_map/all_gather | solution.py:46
  16.2 2.3 copy-start.11
  71.9 1.2 slice-start.6
  179.6 40.2 %copy-start.8 = (f32[512,512]{1,0:T(8,128)}, f32[512,512]{1,0:T(8,128)S(1)}, u32[]{:S(2)}) copy-start(f32[512,512]{1,0:T(8,128)S(1)} %get-tuple-element.245) | copy-start | bytes 3145732
  226.9 10.1 slice-start.4
  228.9 6.8 copy-start
  228.9 8.1 slice-start.5
  235.8 1.3 copy-start.2
  251.1 8.8 slice-start
  256.4 4.1 slice-start.1
  259.9 15.3 %copy-start.3 = (f32[512,4096]{0,1:T(8,128)}, f32[512,4096]{0,1:T(8,128)S(1)}, u32[]{:S(2)}) copy-start(f32[512,4096]{0,1:T(8,128)S(1)} %get-tuple-element.74) | copy-start | bytes 25165828
  298.9 99.0 %all-to-all-start = ((f32[8,512,2,256]{3,2,1,0:T(2,128)}), f32[8,512,2,256]{3,2,1,0:T(2,128)}, u32[]{:S(2)}, u32[]{:S(2)}) async-start(f32[8,512,2,256]{3,2,1,0:T(2,128)} %copy.99), calls=%async_computation | async-start | bytes 16777216 | tf_op jit(solution)/shard_map/all_to_all | solution.py:64
  442.9 129.2 %all-to-all-start.1 = ((f32[16,256,512]{2,1,0:T(8,128)}), f32[16,256,512]{2,1,0:T(8,128)}, u32[]{:S(2)}, u32[]{:S(2)}) async-start(f32[16,256,512]{2,1,0:T(8,128)} %copy.101), calls=%async_computation.1 | async-start | bytes 16777216 | tf_op jit(solution)/shard_map/all_to_all | solution.py:72
  449.7 288.3 %all-reduce.7.cloned.1.call-start = ((), (), s32[]{:S(2)}) async-start(), calls=%async_computation.3 | async-start | bytes 4718592 | tf_op jit(solution)/shard_map/psum | solution.py:16
  669.6 2.2 copy-start.1
  673.3 200.4 %all-reduce.9.cloned.1.call-start = ((), (), s32[]{:S(2)}) async-start(), calls=%async_computation.4 | async-start | bytes 14155776 | tf_op jit(solution)/shard_map/psum | solution.py:16
  873.7 3.6 copy-start.4
  879.3 1.5 copy-start.7
  1105.3 3.8 copy-start.5
  1108.5 2.8 copy-start.6
  1116.2 1.7 copy-start.9
  1116.2 2.4 copy-start.10
  1126.6 6.0 slice-start.2
  1128.5 4.2 slice-start.3
Sparse Core Ops, SparseCore 0:
  18.6 53.2 all-gather.1
  673.5 64.4 all-reduce.6
  742.7 130.9 all-reduce.8
where the time goes:
time: 1170 us; the launch traced here: 1160 us
  waiting for transfers between devices  455 us (39%)
  other arithmetic  335 us (29%)
  matrix products  191 us (16%)
  local copies, waits for them, and re-layouts  146 us (12%)
  between operations  21.7 us (2%)
  starting transfers between devices  12.2 us (1%)
    psum x2, waiting for transfers between devices, spread_2(): return lax.psum(jnp.where(mine, shard, jnp.zeros_like(shard)), axis)  193 us
    another operation x23, other arithmetic, per_device(): parent_pivot = jnp.linalg.cholesky(received[0])  124 us
    all_to_all x1, waiting for transfers between devices, per_device(): lax.all_to_all(outgoing_rows, 'leaf', split_axis=0, concat_axis=0, tiled=...  115 us
    another operation x6, other arithmetic, solve_rows(): return jax.scipy.linalg.solve_triangular(factor, rows.T, lower=True).T  102 us
    all_to_all x1, waiting for transfers between devices, per_device(): lax.all_to_all(outgoing, 'col', split_axis=0, concat_axis=0, tiled=True)  93.7 us
    another operation x14, other arithmetic, per_device(): pivot_factor = jnp.linalg.cholesky(whole_panel[:pivot_width])  89 us
    all_gather x1, waiting for transfers between devices, per_device(): whole_panel = lax.all_gather(raw_panel, 'col', axis=0, tiled=True)  53.1 us
    another operation x29, matrix products, solve_rows(): return jax.scipy.linalg.solve_triangular(factor, rows.T, lower=True).T  51.5 us
  transfers between devices with their start and end apart: 5, of which 5 were waited for; matrix products, arithmetic and copies ran while one was open for 1% of the time, Pallas kernels for 0%

commit v1 on v0

--- a/solution.py
+++ b/solution.py
@@ -18,6 +18,11 @@
 
 def solve_rows(factor, rows):
     return jax.scipy.linalg.solve_triangular(factor, rows.T, lower=True).T
+
+
+def lower_inverse(factor):
+    eye = jnp.eye(factor.shape[0], dtype=factor.dtype)
+    return jax.scipy.linalg.solve_triangular(factor, eye, lower=True)
 
 
 def route_slots(indices, col_blocks):
@@ -45,7 +50,10 @@
     raw_panel = front_rows[:, :pivot_width]
     whole_panel = lax.all_gather(raw_panel, "col", axis=0, tiled=True)
     pivot_factor = jnp.linalg.cholesky(whole_panel[:pivot_width])
-    solved_all = solve_rows(pivot_factor, whole_panel)
+    pivot_inverse = lower_inverse(pivot_factor)
+    solved_all = jnp.dot(
+        whole_panel, pivot_inverse.T, precision=highest, preferred_element_type=jnp.float32
+    )
     own_rows = lax.dynamic_slice_in_dim(solved_all, col_pos * row_count, row_count, 0)
     first_device = col_pos == 0
     child_out = jnp.where(first_device, pivot_factor, own_rows)[None]
@@ -55,6 +63,23 @@
     update_rows = jnp.where(first_device, 0.0, update_rows)
     col_blocks = ROWBLK * leaf_count // col_count
     own_index = lax.dynamic_index_in_dim(child_index, leaf_pos, 0, keepdims=False)
+    parent_pivots = ROWBLK * B
+    block_rows = row_count // B
+    diag = jnp.zeros((ROWBLK, B, B), jnp.float32)
+    for local in range(block_rows):
+        block = jnp.clip((col_pos - 1) * block_rows + local, 0, contrib_count - 1)
+        piece = lax.dynamic_slice(update_rows, (local * B, block * B), (B, B))
+        place = lax.dynamic_index_in_dim(own_index, block, 0, keepdims=False)
+        hit = (jnp.arange(ROWBLK, dtype=jnp.int32) == place) & (col_pos >= 1)
+        diag = diag + jnp.where(hit[:, None, None], piece[None], 0.0)
+    diag_full = jnp.zeros((parent_pivots, parent_pivots), jnp.float32)
+    for p in range(ROWBLK):
+        diag_full = lax.dynamic_update_slice(diag_full, diag[p], (p * B, p * B))
+    corner = (leaf_pos == 0) & (col_pos == 0)
+    early = diag_full + jnp.where(corner, parent_front[:, :parent_pivots], 0.0)
+    pivot_block = lax.psum(early, ("leaf", "col"))
+    parent_pivot = jnp.linalg.cholesky(pivot_block)
+    parent_inverse = lower_inverse(parent_pivot)
     target, ranking = route_slots(own_index, col_blocks)
     slot_ids = jnp.arange(col_count * share, dtype=jnp.int32)
     selector = (slot_ids[:, None] == (target * share + ranking)[None, :]).astype(jnp.float32)
@@ -88,18 +113,22 @@
         axis=1,
     )
     arrived_blocks = arrived.reshape(children, B, share, B)
-    spread = jnp.einsum("gsq,gbse->gbqe", col_select, arrived_blocks, precision=highest)
-    update = jnp.einsum("gp,gbqe->pbqe", row_place, spread, precision=highest)
+    place_map = jnp.einsum("gp,gsq->gspq", row_place, col_select)
+    update = jnp.einsum("gspq,gbse->pbqe", place_map, arrived_blocks, precision=highest)
     assembled = parent_front + update.reshape(ROWBLK * B, col_blocks * B)
-    parent_pivots = ROWBLK * B
     raw_rows = spread_2(assembled[:, :parent_pivots], "col", 0)
     received = []
-    for turn in range(share + 1):
-        root = col_pos * 0 if turn == 0 else col_pos * share + turn - 1
-        received.append(spread_2(raw_rows, "leaf", root))
-    parent_pivot = jnp.linalg.cholesky(received[0])
-    row_panel = solve_rows(parent_pivot, raw_rows)
-    col_panel = solve_rows(parent_pivot, jnp.concatenate(received[1:], 0))
+    for turn in range(share):
+        received.append(spread_2(raw_rows, "leaf", col_pos * share + turn))
+    row_panel = jnp.dot(
+        raw_rows, parent_inverse.T, precision=highest, preferred_element_type=jnp.float32
+    )
+    col_panel = jnp.dot(
+        jnp.concatenate(received, 0),
+        parent_inverse.T,
+        precision=highest,
+        preferred_element_type=jnp.float32,
+    )
     schur = assembled - jnp.dot(
         row_panel, col_panel.T, precision=highest, preferred_element_type=jnp.float32
     )

time: 1170 us -> 1090 us (0.932)
  matrix products: 191 us -> 149 us
  waiting for transfers between devices: 455 us -> 415 us
    psum x0 -> x1, waiting for transfers between devices: none -> 232 us  [per_device(): pivot_block = lax.psum(early, ('leaf', 'col'))]
    psum x2, waiting for transfers between devices: 193 us -> 42.6 us  [spread_2(): return lax.psum(jnp.where(mine, shard, jnp.zeros_like(shard)), axis)]
    all_to_all x1, waiting for transfers between devices: 115 us -> 0.01 us  [per_device(): lax.all_to_all(outgoing_rows, 'leaf', split_axis=0, concat_axis=0, tiled=...]
    another operation x39 -> x28, matrix products: 63.3 us -> 29.2 us  [the longest x18 17.1 us: lower_inverse(): return jax.scipy.linalg.solve_triangular(factor, eye, lower=True)]
    another operation x66 -> x63, local copies, waits for them, and re-layouts: 41.5 us -> 33.2 us
    dot_general x2 -> x4, matrix products: 71.3 us -> 64.6 us  [the longest x1 25.1 us: per_device(): jnp.dot(jnp.concatenate(received, 0), parent_inverse.T, precision=highest...]
    unnamed x40 -> x32, local copies, waits for them, and re-layouts: 33 us -> 30.6 us
  transfers between devices with their start and end apart: 5 -> 6, of which waited for: 5 -> 4; matrix products, arithmetic and copies ran while one was open for 1% -> 26% of each run, Pallas kernels for 0% -> 0%
where the time goes in v1:
time: 1090 us; the launch traced here: 1070 us
  waiting for transfers between devices  415 us (38%)
  other arithmetic  329 us (30%)
  matrix products  149 us (14%)
  local copies, waits for them, and re-layouts  147 us (13%)
  between operations  21.1 us (2%)
  starting transfers between devices  12.5 us (1%)
    psum x1, waiting for transfers between devices, per_device(): pivot_block = lax.psum(early, ('leaf', 'col'))  232 us
    another operation x23, other arithmetic, per_device(): parent_pivot = jnp.linalg.cholesky(pivot_block)  124 us
    another operation x6, other arithmetic, lower_inverse(): return jax.scipy.linalg.solve_triangular(factor, eye, lower=True)  102 us
    all_to_all x1, waiting for transfers between devices, per_device(): lax.all_to_all(outgoing, 'col', split_axis=0, concat_axis=0, tiled=True)  87.6 us
    another operation x14, other arithmetic, per_device(): pivot_factor = jnp.linalg.cholesky(whole_panel[:pivot_width])  78.9 us
    all_gather x1, waiting for transfers between devices, per_device(): whole_panel = lax.all_gather(raw_panel, 'col', axis=0, tiled=True)  52.2 us
    psum x2, waiting for transfers between devices, spread_2(): return lax.psum(jnp.where(mine, shard, jnp.zeros_like(shard)), axis)  42.6 us
    another operation x42, local copies, waits for them, and re-layouts  32.2 us
  transfers between devices with their start and end apart: 6, of which 4 were waited for; matrix products, arithmetic and copies ran while one was open for 26% of the time, Pallas kernels for 0%

profile of v1, /device:TPU:1, one launch (start us, length us, event | category | flops | bytes accessed | tf_op | source)
XLA Modules:
  0.0 1072.9 jit_solution(10194285213609058955)
XLA Ops:
  7.2 9.0 copy.116
  16.2 2.3 slice.309
  19.7 52.2 %all-gather.2.cloned.1.call-done = f32[4096,512]{0,1:T(8,128)} async-done(((f32[512,512]{0,1:T(8,128)}), f32[4096,512]{0,1:T(8,128)}) %all-gather.2.cloned.1.call-update) | async-done | bytes 8388624 | tf_op jit(solution)/shard_map/all_gather | solution.py:51
  74.9 11.7 %cholesky.221 = f32[128,128]{1,0:T(8,128)S(1)} custom-call(f32[128,128]{1,0:T(8,128)S(1)} %cholesky.570), custom_call_target="Cholesky" | custom-call | tf_op jit(solution)/shard_map/jit(cholesky)/cholesky | solution.py:52
  86.8 9.8 custom-call.64
  97.3 11.7 %cholesky.235 = f32[128,128]{1,0:T(8,128)S(1)} custom-call(f32[128,128]{1,0:T(8,128)S(1)} %cholesky.574), custom_call_target="Cholesky" | custom-call | tf_op jit(solution)/shard_map/jit(cholesky)/cholesky | solution.py:52
  109.1 10.1 custom-call.65
  119.9 11.7 %cholesky.254 = f32[128,128]{1,0:T(8,128)S(1)} custom-call(f32[128,128]{1,0:T(8,128)S(1)} %cholesky.579), custom_call_target="Cholesky" | custom-call | tf_op jit(solution)/shard_map/jit(cholesky)/cholesky | solution.py:52
  131.6 9.8 custom-call.66
  142.0 11.9 %cholesky.462 = f32[128,128]{1,0:T(8,128)S(1)} custom-call(f32[128,128]{1,0:T(8,128)S(1)} %convolution_subtract_fusion.14), custom_call_target="Cholesky" | custom-call | tf_op jit(solution)/shard_map/jit(cholesky)/cholesky | solution.py:52
  158.6 10.6 while.2
  169.1 40.1 %custom-call.57 = f32[4,128,128]{1,2,0:T(8,128)S(1)} custom-call(f32[4,128,128]{2,1,0:T(8,128)} %get-tuple-element.12), custom_call_target="InvertDiagBlocksLowerTriangular" | custom-call | tf_op jit(solution)/shard_map/jit(_solve_triangular)/triangular_solve | solution.py:25
  213.1 16.7 %fusion.36 = f32[512,4096]{1,0:T(8,128)S(1)} fusion(f32[4096,512]{0,1:T(8,128)} %all-gather.2.cloned.1.call-done, f32[128,512]{1,0:T(8,128)S(1)} %fusion.97, f32[128,512]{1,0:T(8,128)S(1)} %fusion.98, f32[128,512]{1,0:T(8,128)S(1)} %fusion.100, f32[128,512]{1,0:T(8,128)S(1)} %fusion.75), kind=kOutput, calls=%fused_computation.71 | convolution fusion | flops 12885688320 | bytes 17825792 | tf_op jit(solution)/shard_map/dot_general | solution.py:54
  230.0 15.2 %fusion.4 = f32[512,3584]{0,1:T(8,128)} fusion(f32[512,4096]{0,1:T(8,128)S(1)} %bitcast.220, f32[512,512]{1,0:T(8,128)S(1)} %constant_dynamic-slice_fusion.5, f32[4096,512]{0,1:T(8,128)S(1)} %bitcast.221, pred[]{:T(512)S(6)} %eq.181), kind=kOutput, calls=%fused_computation.9 | convolution fusion | flops 11277959168 | bytes 23068672 | tf_op jit(solution)/shard_map/dot_general | solution.py:60
  245.1 10.1 copy.155
  255.2 6.7 convolution_bitcast_fusion
  261.9 6.9 copy.134
  268.8 5.5 all-to-all-start
  274.4 6.0 copy.123
  280.5 87.6 %all-to-all-done = f32[8,512,2,256]{3,2,1,0:T(2,128)} async-done(((f32[8,512,2,256]{3,2,1,0:T(2,128)}), f32[8,512,2,256]{3,2,1,0:T(2,128)}, u32[]{:S(2)}, u32[]{:S(2)}) %all-to-all-start) | async-done | bytes 8388640 | tf_op jit(solution)/shard_map/all_to_all | solution.py:89
  368.0 8.6 slice.317
  376.6 10.5 reshape.197
  387.1 17.9 %fusion = f32[16,256,512]{2,0,1:T(8,128)S(1)} fusion(f32[14,256,512]{2,1,0:T(8,128)} %reshape.197, s32[14]{0:T(128)S(1)} %fusion.128), kind=kOutput, calls=%fused_computation.4 | convolution fusion | flops 352321760 | bytes 15728696 | tf_op jit(solution)/shard_map/lr,rbx->lbx/dot_general | solution.py:96
  405.0 8.1 copy.136
  413.1 6.8 all-to-all-start.1
  423.9 3.4 fusion.11
  431.7 232.1 %all-reduce.9.cloned.1.call-done = f32[768,768]{0,1:T(8,128)} async-done(((f32[768,768]{0,1:T(8,128)}), f32[768,768]{0,1:T(8,128)}) %all-reduce.9.cloned.1.call-update) | async-done | bytes 2359312 | tf_op jit(solution)/shard_map/psum | solution.py:80
  663.8 3.4 copy.124
  670.6 11.7 %cholesky.474 = f32[128,128]{1,0:T(8,128)S(1)} custom-call(f32[128,128]{1,0:T(8,128)S(1)} %cholesky.583), custom_call_target="Cholesky" | custom-call | tf_op jit(solution)/shard_map/jit(cholesky)/cholesky | solution.py:81
  682.7 9.8 custom-call.58
  695.4 11.7 %cholesky.492 = f32[128,128]{1,0:T(8,128)S(1)} custom-call(f32[128,128]{1,0:T(8,128)S(1)} %cholesky.587), custom_call_target="Cholesky" | custom-call | tf_op jit(solution)/shard_map/jit(cholesky)/cholesky | solution.py:81
  707.3 10.2 custom-call.59
  719.9 11.7 %cholesky.513 = f32[128,128]{1,0:T(8,128)S(1)} custom-call(f32[128,128]{1,0:T(8,128)S(1)} %cholesky.592), custom_call_target="Cholesky" | custom-call | tf_op jit(solution)/shard_map/jit(cholesky)/cholesky | solution.py:81
  731.8 9.8 custom-call.67
  742.0 2.1 convolution_subtract_fusion.9
  744.1 11.9 %cholesky.528 = f32[128,128]{1,0:T(8,128)S(1)} custom-call(f32[128,128]{1,0:T(8,128)S(1)} %cholesky.597), custom_call_target="Cholesky" | custom-call | tf_op jit(solution)/shard_map/jit(cholesky)/cholesky | solution.py:81
  756.1 9.8 custom-call.68
  768.2 11.7 %cholesky.543 = f32[128,128]{1,0:T(8,128)S(1)} custom-call(f32[128,128]{1,0:T(8,128)S(1)} %cholesky.602), custom_call_target="Cholesky" | custom-call | tf_op jit(solution)/shard_map/jit(cholesky)/cholesky | solution.py:81
  780.0 9.8 custom-call.69
  792.1 9.3 copy.137
  801.4 10.5 copy.156
  811.8 9.8 convolution_bitcast_fusion.1
  821.6 6.6 copy.163
  828.3 3.9 copy.167
  832.2 3.0 add.171
  835.2 2.2 copy-done
  839.6 11.7 %cholesky.557 = f32[128,128]{1,0:T(8,128)S(1)} custom-call(f32[128,128]{1,0:T(8,128)S(1)} %convolution_subtract_fusion.13), custom_call_target="Cholesky" | custom-call | tf_op jit(solution)/shard_map/jit(cholesky)/cholesky | solution.py:81
  859.6 42.6 %all-reduce.11.cloned.1.call-done = f32[768,768]{0,1:T(8,128)} async-done(((f32[768,768]{0,1:T(8,128)}), f32[768,768]{0,1:T(8,128)}) %all-reduce.11.cloned.1.call-update) | async-done | bytes 2359312 | tf_op jit(solution)/shard_map/psum | solution.py:16
  902.2 4.2 broadcast_select_fusion.1
  906.4 21.8 %while.3 = (s32[]{:T(128)}, f32[768,768]{0,1:T(8,128)}, s32[6,2]{0,1:T(2,128)S(1)}, f32[6,128,128]{2,1,0:T(8,128)}, s32[]{:T(128)}) while((s32[]{:T(128)}, f32[768,768]{0,1:T(8,128)}, s32[6,2]{0,1:T(2,128)S(1)}, f32[6,128,128]{2,1,0:T(8,128)}, s32[]{:T(128)}) %tuple.83), condition=%wide.while_cond.1, body=%wide.while_body.1.sunk | while | flops 2 | bytes 393329 | solution.py:25
  907.1 2.3 dynamic-slice.23
  910.7 2.3 dynamic-slice.23
  914.4 2.3 dynamic-slice.23
  918.0 2.3 dynamic-slice.23
  921.6 2.3 dynamic-slice.23
  925.3 2.2 dynamic-slice.23
  928.2 59.9 %custom-call.60 = f32[6,128,128]{1,2,0:T(8,128)S(1)} custom-call(f32[6,128,128]{2,1,0:T(8,128)} %get-tuple-element.20), custom_call_target="InvertDiagBlocksLowerTriangular" | custom-call | tf_op jit(solution)/shard_map/jit(_solve_triangular)/triangular_solve | solution.py:25
  996.0 2.0 fusion.23
  998.6 2.5 convolution_subtract_fusion
  1003.1 13.1 %fusion.140 = f32[768,768]{1,0:T(8,128)} fusion(f32[768,768]{0,1:T(8,128)S(1)} %copy-done.3, f32[768,768]{1,0:T(8,128)S(1)} %convolution_dynamic-update-slice_fusion), kind=kOutput, calls=%fused_computation.273 | convolution fusion | flops 5435817984 | bytes 7077888 | tf_op jit(solution)/shard_map/dot_general | solution.py:123
  1016.2 3.1 copy.147
  1021.0 25.1 %fusion.7 = f32[1536,768]{1,0:T(8,128)S(1)} fusion(f32[768,768]{1,0:T(8,128)} %copy-done.7, f32[768,768]{0,1:T(8,128)} %get-tuple-element.67, f32[768,768]{0,1:T(8,128)} %get-tuple-element.68), kind=kOutput, calls=%fused_computation.10 | convolution fusion | flops 10872815616 | bytes 11796480 | tf_op jit(solution)/shard_map/dot_general | solution.py:126
  1046.1 13.8 %select_select_fusion = f32[768,1536]{0,1:T(8,128)} fusion(f32[768,1536]{0,1:T(8,128)S(1)} %bitcast.225, f32[768,768]{0,1:T(8,128)S(1)} %copy-done.4, f32[768,768]{1,0:T(8,128)S(1)} %copy-done.1, f32[1536,768]{1,0:T(8,128)S(1)} %fusion.7, pred[1536]{0:T(1024)(128)(4,1)S(1)} %add_compare_fusion, pred[768]{0:T(1024)(128)(4,1)S(1)} %add_compare_fusion.1), kind=kOutput, calls=%fused_computation.14 | convolution fusion | flops 10875174912 | bytes 18876672 | tf_op jit(solution)/shard_map/dot_general | solution.py:132
  1059.9 6.0 copy.149
  (196 shorter events, 73.0 us)
Async XLA Ops:
  7.2 64.7 %all-gather.2.cloned.1.call-start = ((), (), s32[]{:S(2)}) async-start(), calls=%async_computation.2 | async-start | bytes 9437184 | tf_op jit(solution)/shard_map/all_gather | solution.py:51
  16.2 2.3 copy-start.8
  71.9 1.2 slice-start.4
  212.7 17.3 %slice-start = ((s8[8388608]{0:T(1024)(128)(4,1)}), s8[4194304]{0:T(1024)(128)(4,1)S(1)}, s32[]{:S(2)}) async-start(s8[8388608]{0:T(1024)(128)(4,1)} %bitcast.218), calls=%async_computation.6 | async-start | bytes 8388608
  213.1 16.8 %slice-start.1 = ((s8[8388608]{0:T(1024)(128)(4,1)}), s8[4194304]{0:T(1024)(128)(4,1)S(1)}, s32[]{:S(2)}) async-start(s8[8388608]{0:T(1024)(128)(4,1)} %bitcast.218), calls=%async_computation.7 | async-start | bytes 8388608
  268.8 99.2 %all-to-all-start = ((f32[8,512,2,256]{3,2,1,0:T(2,128)}), f32[8,512,2,256]{3,2,1,0:T(2,128)}, u32[]{:S(2)}, u32[]{:S(2)}) async-start(f32[8,512,2,256]{3,2,1,0:T(2,128)} %copy.134), calls=%async_computation | async-start | bytes 16777216 | tf_op jit(solution)/shard_map/all_to_all | solution.py:89
  413.1 379.0 %all-to-all-start.1 = ((f32[16,256,512]{2,1,0:T(8,128)}), f32[16,256,512]{2,1,0:T(8,128)}, u32[]{:S(2)}, u32[]{:S(2)}) async-start(f32[16,256,512]{2,1,0:T(8,128)} %copy.136), calls=%async_computation.1 | async-start | bytes 16777216 | tf_op jit(solution)/shard_map/all_to_all | solution.py:97
  419.8 244.0 %all-reduce.9.cloned.1.call-start = ((), (), s32[]{:S(2)}) async-start(), calls=%async_computation.3 | async-start | bytes 4718592 | tf_op jit(solution)/shard_map/psum | solution.py:80
  427.4 474.8 %all-reduce.11.cloned.1.call-start = ((), (), s32[]{:S(2)}) async-start(), calls=%async_computation.4 | async-start | bytes 4718592 | tf_op jit(solution)/shard_map/psum | solution.py:16
  663.8 3.4 copy-start.2
  669.2 1.4 copy-start.6
  835.2 2.2 copy-start
  838.9 182.0 %all-reduce.13.cloned.1.call-start = ((), (), s32[]{:S(2)}) async-start(), calls=%async_computation.5 | async-start | bytes 9437184 | tf_op jit(solution)/shard_map/psum | solution.py:16
  988.1 3.4 copy-start.5
  998.1 5.1 copy-start.3
  1001.6 1.5 copy-start.7
  1019.3 26.8 %slice-start.2 = ((s8[4718592]{0:T(1024)(128)(4,1)}), s8[524288]{0:T(1024)(128)(4,1)S(1)}, s32[]{:S(2)}) async-start(s8[4718592]{0:T(1024)(128)(4,1)} %bitcast.224), calls=%async_computation.8 | async-start | bytes 1048576
  1020.9 25.1 %slice-start.3 = ((s8[4718592]{0:T(1024)(128)(4,1)}), s8[4194304]{0:T(1024)(128)(4,1)S(1)}, s32[]{:S(2)}) async-start(s8[4718592]{0:T(1024)(128)(4,1)} %bitcast.224), calls=%async_computation.9 | async-start | bytes 8388608
  1020.9 25.1 %copy-start.1 = (f32[768,768]{1,0:T(8,128)S(1)}, f32[768,768]{1,0:T(8,128)}, u32[]{:S(2)}) copy-start(f32[768,768]{1,0:T(8,128)} %fusion.140) | copy-start | bytes 7077892
  1020.9 25.1 %copy-start.4 = (f32[768,768]{0,1:T(8,128)S(1)}, f32[768,768]{0,1:T(8,128)}, u32[]{:S(2)}) copy-start(f32[768,768]{0,1:T(8,128)} %fusion.14) | copy-start | bytes 7077892
Sparse Core Ops, SparseCore 0:
  18.6 53.2 all-gather.1
  427.5 236.3 all-reduce.8
  839.0 63.1 all-reduce.10
  906.5 109.9 all-reduce.12

commit v2 on v1

--- a/solution.py
+++ b/solution.py
@@ -49,6 +49,9 @@
     pivot_width = PC * B
     raw_panel = front_rows[:, :pivot_width]
     whole_panel = lax.all_gather(raw_panel, "col", axis=0, tiled=True)
+    corner = (leaf_pos == 0) & (col_pos == 0)
+    parent_pivots = ROWBLK * B
+    front_pivot = jnp.where(corner, parent_front[:, :parent_pivots], 0.0)
     pivot_factor = jnp.linalg.cholesky(whole_panel[:pivot_width])
     pivot_inverse = lower_inverse(pivot_factor)
     solved_all = jnp.dot(
@@ -63,21 +66,23 @@
     update_rows = jnp.where(first_device, 0.0, update_rows)
     col_blocks = ROWBLK * leaf_count // col_count
     own_index = lax.dynamic_index_in_dim(child_index, leaf_pos, 0, keepdims=False)
-    parent_pivots = ROWBLK * B
     block_rows = row_count // B
     diag = jnp.zeros((ROWBLK, B, B), jnp.float32)
     for local in range(block_rows):
         block = jnp.clip((col_pos - 1) * block_rows + local, 0, contrib_count - 1)
-        piece = lax.dynamic_slice(update_rows, (local * B, block * B), (B, B))
+        source = lax.dynamic_slice(front_rows, (local * B, pivot_width + block * B), (B, B))
+        solved = own_rows[local * B : (local + 1) * B]
+        piece = source - jnp.dot(
+            solved, solved.T, precision=highest, preferred_element_type=jnp.float32
+        )
         place = lax.dynamic_index_in_dim(own_index, block, 0, keepdims=False)
         hit = (jnp.arange(ROWBLK, dtype=jnp.int32) == place) & (col_pos >= 1)
         diag = diag + jnp.where(hit[:, None, None], piece[None], 0.0)
-    diag_full = jnp.zeros((parent_pivots, parent_pivots), jnp.float32)
+    diag_full = front_pivot
     for p in range(ROWBLK):
-        diag_full = lax.dynamic_update_slice(diag_full, diag[p], (p * B, p * B))
-    corner = (leaf_pos == 0) & (col_pos == 0)
-    early = diag_full + jnp.where(corner, parent_front[:, :parent_pivots], 0.0)
-    pivot_block = lax.psum(early, ("leaf", "col"))
+        corner_block = lax.dynamic_slice(diag_full, (p * B, p * B), (B, B))
+        diag_full = lax.dynamic_update_slice(diag_full, corner_block + diag[p], (p * B, p * B))
+    pivot_block = lax.psum(diag_full, ("leaf", "col"))
     parent_pivot = jnp.linalg.cholesky(pivot_block)
     parent_inverse = lower_inverse(parent_pivot)
     target, ranking = route_slots(own_index, col_blocks)
@@ -86,6 +91,7 @@
     selector = selector.reshape(col_count, share, contrib_count)
     pieces = update_rows.reshape(row_count, contrib_count, B)
     outgoing = jnp.einsum("msc,rcb->mrsb", selector, pieces, precision=highest)
+    outgoing = outgoing + pivot_block[0, 0] * 0.0
     incoming = lax.all_to_all(outgoing, "col", split_axis=0, concat_axis=0, tiled=True)
     columns = incoming.reshape(col_count * row_count, share * B)
     contrib_rows = columns[pivot_width:].reshape(contrib_count, B, share * B)
@@ -94,6 +100,7 @@
         jnp.float32
     )
     outgoing_rows = jnp.einsum("lr,rbx->lbx", row_select, contrib_rows, precision=highest)
+    outgoing_rows = outgoing_rows + parent_pivot[0, 0] * 0.0
     arrived = lax.all_to_all(outgoing_rows, "leaf", split_axis=0, concat_axis=0, tiled=True)
     all_target, all_rank = route_slots(child_index, col_blocks)
     local_col = child_index - col_pos * col_blocks
@@ -112,7 +119,7 @@
         ),
         axis=1,
     )
-    arrived_blocks = arrived.reshape(children, B, share, B)
+    arrived_blocks = arrived.reshape(children, B, share, B) + parent_inverse[0, 0] * 0.0
     place_map = jnp.einsum("gp,gsq->gspq", row_place, col_select)
     update = jnp.einsum("gspq,gbse->pbqe", place_map, arrived_blocks, precision=highest)
     assembled = parent_front + update.reshape(ROWBLK * B, col_blocks * B)

time: 1090 us -> 1070 us (0.982)
  waiting for transfers between devices: 415 us -> 350 us
  other arithmetic: 329 us -> 355 us
  matrix products: 149 us -> 163 us
  local copies, waits for them, and re-layouts: 147 us -> 158 us
    psum x1, waiting for transfers between devices: 232 us -> 124 us  [per_device(): pivot_block = lax.psum(diag_full, ('leaf', 'col'))]
    psum x2, waiting for transfers between devices: 42.6 us -> 140 us  [spread_2(): return lax.psum(jnp.where(mine, shard, jnp.zeros_like(shard)), axis)]
    all_to_all x1, waiting for transfers between devices: 87.6 us -> 0.01 us  [per_device(): lax.all_to_all(outgoing, 'col', split_axis=0, concat_axis=0, tiled=True)]
    all_to_all x1, waiting for transfers between devices: 0.01 us -> 44.7 us  [per_device(): lax.all_to_all(outgoing_rows, 'leaf', split_axis=0, concat_axis=0, tiled=...]
    add x0 -> x3, local copies, waits for them, and re-layouts: none -> 25.4 us  [the longest x1 10.5 us: per_device(): arrived.reshape(children, B, share, B) + parent_inverse[0, 0] * 0.0]
    another operation x23, other arithmetic: 124 us -> 137 us  [per_device(): parent_pivot = jnp.linalg.cholesky(pivot_block)]
    all_gather x1, waiting for transfers between devices: 52.2 us -> 40.6 us  [per_device(): whole_panel = lax.all_gather(raw_panel, 'col', axis=0, tiled=True)]
    unnamed x32 -> x48, local copies, waits for them, and re-layouts: 30.6 us -> 37.6 us
  transfers between devices with their start and end apart: 6 -> 6, of which waited for: 4 -> 5; matrix products, arithmetic and copies ran while one was open for 26% -> 30% of each run, Pallas kernels for 0% -> 0%
where the time goes in v2:
time: 1070 us; the launch traced here: 1060 us
  other arithmetic  355 us (33%)
  waiting for transfers between devices  350 us (33%)
  matrix products  163 us (15%)
  local copies, waits for them, and re-layouts  158 us (15%)
  between operations  23.2 us (2%)
  starting transfers between devices  11.6 us (1%)
    psum x2, waiting for transfers between devices, spread_2(): return lax.psum(jnp.where(mine, shard, jnp.zeros_like(shard)), axis)  140 us
    another operation x23, other arithmetic, per_device(): parent_pivot = jnp.linalg.cholesky(pivot_block)  137 us
    psum x1, waiting for transfers between devices, per_device(): pivot_block = lax.psum(diag_full, ('leaf', 'col'))  124 us
    another operation x6, other arithmetic, lower_inverse(): return jax.scipy.linalg.solve_triangular(factor, eye, lower=True)  102 us
    another operation x14, other arithmetic, per_device(): pivot_factor = jnp.linalg.cholesky(whole_panel[:pivot_width])  78.9 us
    all_to_all x1, waiting for transfers between devices, per_device(): lax.all_to_all(outgoing_rows, 'leaf', split_axis=0, concat_axis=0, tiled=...  44.7 us
    all_gather x1, waiting for transfers between devices, per_device(): whole_panel = lax.all_gather(raw_panel, 'col', axis=0, tiled=True)  40.6 us
    unnamed x48, local copies, waits for them, and re-layouts  37.6 us
  transfers between devices with their start and end apart: 6, of which 5 were waited for; matrix products, arithmetic and copies ran while one was open for 30% of the time, Pallas kernels for 0%

profile of v2, /device:TPU:1, one launch (start us, length us, event | category | flops | bytes accessed | tf_op | source)
XLA Modules:
  0.0 1060.1 jit_solution(6337166405526484480)
XLA Ops:
  7.2 9.0 copy.128
  16.2 2.3 slice.330
  18.6 6.0 copy.134
  28.0 3.3 slice_select_fusion.1
  31.3 40.6 %all-gather.2.cloned.1.call-done = f32[4096,512]{0,1:T(8,128)} async-done(((f32[512,512]{0,1:T(8,128)}), f32[4096,512]{0,1:T(8,128)}) %all-gather.2.cloned.1.call-update) | async-done | bytes 8388624 | tf_op jit(solution)/shard_map/all_gather | solution.py:51
  74.9 11.7 %cholesky.221 = f32[128,128]{1,0:T(8,128)S(1)} custom-call(f32[128,128]{1,0:T(8,128)S(1)} %cholesky.570), custom_call_target="Cholesky" | custom-call | tf_op jit(solution)/shard_map/jit(cholesky)/cholesky | solution.py:55
  86.7 9.8 custom-call.64
  97.3 11.7 %cholesky.235 = f32[128,128]{1,0:T(8,128)S(1)} custom-call(f32[128,128]{1,0:T(8,128)S(1)} %cholesky.574), custom_call_target="Cholesky" | custom-call | tf_op jit(solution)/shard_map/jit(cholesky)/cholesky | solution.py:55
  109.0 10.1 custom-call.65
  120.9 11.7 %cholesky.254 = f32[128,128]{1,0:T(8,128)S(1)} custom-call(f32[128,128]{1,0:T(8,128)S(1)} %cholesky.579), custom_call_target="Cholesky" | custom-call | tf_op jit(solution)/shard_map/jit(cholesky)/cholesky | solution.py:55
  133.3 9.8 custom-call.66
  144.6 11.8 %cholesky.462 = f32[128,128]{1,0:T(8,128)S(1)} custom-call(f32[128,128]{1,0:T(8,128)S(1)} %convolution_subtract_fusion.16), custom_call_target="Cholesky" | custom-call | tf_op jit(solution)/shard_map/jit(cholesky)/cholesky | solution.py:55
  160.4 10.9 %while.2 = (s32[]{:T(128)}, f32[512,512]{1,0:T(8,128)S(1)}, s32[4,2]{0,1:T(2,128)S(1)}, f32[4,128,128]{2,1,0:T(8,128)}, s32[]{:T(128)}) while((s32[]{:T(128)}, f32[512,512]{1,0:T(8,128)S(1)}, s32[4,2]{0,1:T(2,128)S(1)}, f32[4,128,128]{2,1,0:T(8,128)}, s32[]{:T(128)}) %tuple.80), condition=%wide.while_cond, body=%wide.while_body.sunk | while | flops 2 | bytes 132705 | solution.py:25
  171.3 40.8 %custom-call.57 = f32[4,128,128]{1,2,0:T(8,128)} custom-call(f32[4,128,128]{2,1,0:T(8,128)} %get-tuple-element.12), custom_call_target="InvertDiagBlocksLowerTriangular" | custom-call | tf_op jit(solution)/shard_map/jit(_solve_triangular)/triangular_solve | solution.py:25
  216.9 16.7 %fusion.36 = f32[512,4096]{1,0:T(8,128)S(1)} fusion(f32[4096,512]{0,1:T(8,128)} %all-gather.2.cloned.1.call-done, f32[128,512]{1,0:T(8,128)S(1)} %fusion.102, f32[128,512]{1,0:T(8,128)S(1)} %fusion.103, f32[128,512]{1,0:T(8,128)S(1)} %fusion.105, f32[128,512]{1,0:T(8,128)S(1)} %fusion.80), kind=kOutput, calls=%fused_computation.74 | convolution fusion | flops 12885688320 | bytes 17825792 | tf_op jit(solution)/shard_map/dot_general | solution.py:57
  233.6 3.2 copy-done
  237.2 2.5 convolution_subtract_fusion.8
  240.8 2.3 convolution_subtract_fusion.9
  251.1 17.0 %fusion.4 = f32[512,3584]{0,1:T(8,128)} fusion(f32[512,4096]{0,1:T(8,128)} %bitcast.233, f32[512,512]{1,0:T(8,128)S(1)} %constant_dynamic-slice_fusion.3, f32[4096,512]{0,1:T(8,128)} %bitcast.234, pred[]{:T(512)S(6)} %eq.181), kind=kOutput, calls=%fused_computation.10 | convolution fusion | flops 11277959168 | bytes 23068672 | tf_op jit(solution)/shard_map/dot_general | solution.py:63
  268.1 10.2 copy.170
  278.3 124.3 %all-reduce.8.cloned.1.call-done = f32[768,768]{0,1:T(8,128)} async-done(((f32[768,768]{0,1:T(8,128)}), f32[768,768]{0,1:T(8,128)}) %all-reduce.8.cloned.1.call-update) | async-done | bytes 2359312 | tf_op jit(solution)/shard_map/psum | solution.py:85
  404.3 6.8 add_bitcast_fusion
  411.1 6.9 copy.148
  418.0 6.0 all-to-all-start
  424.0 2.4 copy.137
  429.8 11.7 %cholesky.474 = f32[128,128]{1,0:T(8,128)S(1)} custom-call(f32[128,128]{1,0:T(8,128)S(1)} %cholesky.583), custom_call_target="Cholesky" | custom-call | tf_op jit(solution)/shard_map/jit(cholesky)/cholesky | solution.py:86
  442.3 9.8 custom-call.58
  455.8 11.7 %cholesky.492 = f32[128,128]{1,0:T(8,128)S(1)} custom-call(f32[128,128]{1,0:T(8,128)S(1)} %cholesky.587), custom_call_target="Cholesky" | custom-call | tf_op jit(solution)/shard_map/jit(cholesky)/cholesky | solution.py:86
  469.8 10.8 %custom-call.59 = f32[1,128,128]{1,2,0:T(8,128)S(1)} custom-call(f32[1,128,128]{2,1,0:T(8,128)} %get-tuple-element.99), custom_call_target="InvertDiagBlocksLowerTriangular" | custom-call | tf_op jit(solution)/shard_map/jit(cholesky)/cholesky | solution.py:86
  485.6 11.7 %cholesky.513 = f32[128,128]{1,0:T(8,128)S(1)} custom-call(f32[128,128]{1,0:T(8,128)S(1)} %cholesky.592), custom_call_target="Cholesky" | custom-call | tf_op jit(solution)/shard_map/jit(cholesky)/cholesky | solution.py:86
  498.7 10.6 %custom-call.67 = f32[1,128,128]{1,2,0:T(8,128)S(1)} custom-call(f32[1,128,128]{2,1,0:T(8,128)} %get-tuple-element.97), custom_call_target="InvertDiagBlocksLowerTriangular" | custom-call | tf_op jit(solution)/shard_map/jit(cholesky)/cholesky/custom-call.12 | solution.py:86
  513.4 11.9 %cholesky.528 = f32[128,128]{1,0:T(8,128)S(1)} custom-call(f32[128,128]{1,0:T(8,128)S(1)} %cholesky.597), custom_call_target="Cholesky" | custom-call | tf_op jit(solution)/shard_map/jit(cholesky)/cholesky | solution.py:86
  526.6 10.6 %custom-call.68 = f32[1,128,128]{1,2,0:T(8,128)S(1)} custom-call(f32[1,128,128]{2,1,0:T(8,128)} %get-tuple-element.95), custom_call_target="InvertDiagBlocksLowerTriangular" | custom-call | tf_op jit(solution)/shard_map/jit(cholesky)/cholesky/custom-call.13 | solution.py:86
  541.1 13.2 %cholesky.543 = f32[128,128]{1,0:T(8,128)} custom-call(f32[128,128]{1,0:T(8,128)} %cholesky.602), custom_call_target="Cholesky" | custom-call | tf_op jit(solution)/shard_map/jit(cholesky)/cholesky | solution.py:86
  557.8 11.3 %custom-call.69 = f32[1,128,128]{1,2,0:T(8,128)} custom-call(f32[1,128,128]{2,1,0:T(8,128)} %get-tuple-element.93), custom_call_target="InvertDiagBlocksLowerTriangular" | custom-call | tf_op jit(solution)/shard_map/jit(cholesky)/cholesky/custom-call.14 | solution.py:86
  573.0 11.7 %cholesky.557 = f32[128,128]{1,0:T(8,128)S(1)} custom-call(f32[128,128]{1,0:T(8,128)S(1)} %convolution_subtract_fusion.15), custom_call_target="Cholesky" | custom-call | tf_op jit(solution)/shard_map/jit(cholesky)/cholesky | solution.py:86
  599.3 8.6 slice.341
  607.9 10.5 reshape.205
  618.4 19.1 %broadcast_add_fusion.1 = f32[16,256,512]{2,0,1:T(8,128)S(1)} fusion(f32[]{:T(128)} %bitcast.51, f32[14,256,512]{2,1,0:T(8,128)} %reshape.205, s32[14]{0:T(128)S(1)} %fusion.133), kind=kOutput, calls=%fused_computation.17 | convolution fusion | flops 354418912 | bytes 15728700 | tf_op jit(solution)/shard_map/lr,rbx->lbx/dot_general | solution.py:102
  637.4 8.1 copy.150
  645.5 4.8 all-to-all-start.1
  651.7 17.8 %while.3 = (s32[]{:T(128)}, f32[768,768]{0,1:T(8,128)}, s32[6,2]{0,1:T(2,128)S(1)}, f32[6,128,128]{2,1,0:T(8,128)S(1)}, s32[]{:T(128)}) while((s32[]{:T(128)}, f32[768,768]{0,1:T(8,128)}, s32[6,2]{0,1:T(2,128)S(1)}, f32[6,128,128]{2,1,0:T(8,128)S(1)}, s32[]{:T(128)}) %tuple.83), condition=%wide.while_cond.1, body=%wide.while_body.1.sunk | while | flops 2 | bytes 393321 | solution.py:25
  652.4 2.2 dynamic-slice.25
  655.3 2.2 dynamic-slice.25
  658.3 2.2 dynamic-slice.25
  661.3 2.2 dynamic-slice.25
  669.5 59.0 %custom-call.60 = f32[6,128,128]{1,2,0:T(8,128)S(1)} custom-call(f32[6,128,128]{2,1,0:T(8,128)S(1)} %get-tuple-element.20), custom_call_target="InvertDiagBlocksLowerTriangular" | custom-call | tf_op jit(solution)/shard_map/jit(_solve_triangular)/triangular_solve | solution.py:25
  731.0 44.7 %all-to-all-done.1 = f32[16,256,512]{2,1,0:T(8,128)} async-done(((f32[16,256,512]{2,1,0:T(8,128)}), f32[16,256,512]{2,1,0:T(8,128)}, u32[]{:S(2)}, u32[]{:S(2)}) %all-to-all-start.1) | async-done | bytes 8388640 | tf_op jit(solution)/shard_map/all_to_all | solution.py:104
  775.7 9.3 copy.153
  784.9 7.3 broadcast_add_fusion
  792.2 10.5 copy.171
  802.7 9.8 convolution_bitcast_fusion
  812.5 6.6 copy.178
  819.1 3.9 copy.183
  823.0 3.0 add.221
  830.3 63.5 %all-reduce.10.cloned.1.call-done = f32[768,768]{0,1:T(8,128)} async-done(((f32[768,768]{0,1:T(8,128)}), f32[768,768]{0,1:T(8,128)}) %all-reduce.10.cloned.1.call-update) | async-done | bytes 2359312 | tf_op jit(solution)/shard_map/psum | solution.py:16
  893.8 4.1 broadcast_select_fusion.1
  909.8 2.5 convolution_subtract_fusion
  914.3 11.7 %fusion.145 = f32[768,768]{1,0:T(8,128)S(1)} fusion(f32[768,768]{0,1:T(8,128)S(1)} %copy-done.4, f32[768,768]{1,0:T(8,128)S(1)} %convolution_dynamic-update-slice_fusion), kind=kOutput, calls=%fused_computation.279 | convolution fusion | flops 5435817984 | bytes 7077888 | tf_op jit(solution)/shard_map/dot_general | solution.py:130
  928.0 3.4 broadcast_select_fusion.2
  931.4 76.5 %all-reduce.12.cloned.1.call-done = (f32[768,768]{0,1:T(8,128)}, f32[768,768]{0,1:T(8,128)}) async-done(((f32[768,768]{0,1:T(8,128)}, f32[768,768]{0,1:T(8,128)}), (f32[768,768]{0,1:T(8,128)}, f32[768,768]{0,1:T(8,128)})) %all-reduce.12.cloned.1.call-update) | async-done | bytes 4718608 | tf_op jit(solution)/shard_map/psum | solution.py:16
  1007.9 25.3 %fusion.7 = f32[1536,768]{1,0:T(8,128)S(1)} fusion(f32[768,768]{1,0:T(8,128)} %copy-done.10, f32[768,768]{0,1:T(8,128)} %get-tuple-element.67, f32[768,768]{0,1:T(8,128)} %get-tuple-element.68), kind=kOutput, calls=%fused_computation.11 | convolution fusion | flops 10872815616 | bytes 11796480 | tf_op jit(solution)/shard_map/dot_general | solution.py:133
  1033.2 13.9 %select_select_fusion = f32[768,1536]{0,1:T(8,128)} fusion(f32[768,1536]{0,1:T(8,128)S(1)} %bitcast.236, f32[768,768]{0,1:T(8,128)S(1)} %copy-done.5, f32[768,768]{1,0:T(8,128)S(1)} %fusion.145, f32[1536,768]{1,0:T(8,128)S(1)} %fusion.7, pred[1536]{0:T(1024)(128)(4,1)S(1)} %add_compare_fusion, pred[768]{0:T(1024)(128)(4,1)S(1)} %add_compare_fusion.1), kind=kOutput, calls=%fused_computation.15 | convolution fusion | flops 10875174912 | bytes 18876672 | tf_op jit(solution)/shard_map/dot_general | solution.py:139
  1047.1 6.0 copy.164
  (217 shorter events, 114.2 us)
Async XLA Ops:
  7.2 64.7 %all-gather.2.cloned.1.call-start = ((), (), s32[]{:S(2)}) async-start(), calls=%async_computation.2 | async-start | bytes 9437184 | tf_op jit(solution)/shard_map/all_gather | solution.py:51
  18.5 384.0 %all-reduce.8.cloned.1.call-start = ((), (), s32[]{:S(2)}) async-start(), calls=%async_computation.3 | async-start | bytes 4718592 | tf_op jit(solution)/shard_map/psum | solution.py:85
  18.6 6.1 copy-start.18
  71.9 1.2 slice-start.2
  74.9 44.3 %copy-start.13 = (f32[512,512]{1,0:T(8,128)}, f32[512,512]{1,0:T(8,128)S(1)}, u32[]{:S(2)}) copy-start(f32[512,512]{1,0:T(8,128)S(1)} %fusion.44) | copy-start | bytes 3145732
  119.5 93.8 %copy-start.11 = (f32[512,512]{1,0:T(8,128)S(1)}, f32[512,512]{1,0:T(8,128)}, u32[]{:S(2)}) copy-start(f32[512,512]{1,0:T(8,128)} %fusion.69) | copy-start | bytes 3145732
  212.1 3.3 copy-start.17
  233.6 3.2 copy-start
  237.2 10.4 copy-start.6
  418.0 6.1 copy-start.3
  418.0 181.3 %all-to-all-start = ((f32[8,512,2,256]{3,2,1,0:T(2,128)}), f32[8,512,2,256]{3,2,1,0:T(2,128)}, u32[]{:S(2)}, u32[]{:S(2)}) async-start(f32[8,512,2,256]{3,2,1,0:T(2,128)} %copy.148), calls=%async_computation | async-start | bytes 16777216 | tf_op jit(solution)/shard_map/all_to_all | solution.py:95
  428.4 1.4 copy-start.8
  455.8 11.7 %copy-start.14 = (f32[640,128]{1,0:T(8,128)}, f32[640,128]{1,0:T(8,128)S(1)}, u32[]{:S(2)}) copy-start(f32[640,128]{1,0:T(8,128)S(1)} %convolution_subtract_fusion.4) | copy-start | bytes 983044
  484.9 0.7 copy-start.15
  512.7 0.7 copy-start.16
  596.7 1.4 copy-start.2
  645.5 130.1 %all-to-all-start.1 = ((f32[16,256,512]{2,1,0:T(8,128)}), f32[16,256,512]{2,1,0:T(8,128)}, u32[]{:S(2)}, u32[]{:S(2)}) async-start(f32[16,256,512]{2,1,0:T(8,128)} %copy.150), calls=%async_computation.1 | async-start | bytes 16777216 | tf_op jit(solution)/shard_map/all_to_all | solution.py:104
  650.3 243.5 %all-reduce.10.cloned.1.call-start = ((), (), s32[]{:S(2)}) async-start(), calls=%async_computation.4 | async-start | bytes 4718592 | tf_op jit(solution)/shard_map/psum | solution.py:16
  826.0 2.2 copy-start.1
  829.9 178.0 %all-reduce.12.cloned.1.call-start = ((), (), s32[]{:S(2)}) async-start(), calls=%async_computation.5 | async-start | bytes 9437184 | tf_op jit(solution)/shard_map/psum | solution.py:16
  898.0 1.2 copy-start.7
  899.2 3.1 copy-start.9
  899.2 3.1 copy-start.12
  909.3 5.1 copy-start.4
  912.8 1.5 copy-start.10
  928.0 105.2 %slice-start = ((s8[4718592]{0:T(1024)(128)(4,1)}), s8[524288]{0:T(1024)(128)(4,1)S(1)}, s32[]{:S(2)}) async-start(s8[4718592]{0:T(1024)(128)(4,1)} %bitcast.235), calls=%async_computation.6 | async-start | bytes 1048576
  1007.9 25.3 %slice-start.1 = ((s8[4718592]{0:T(1024)(128)(4,1)}), s8[4194304]{0:T(1024)(128)(4,1)S(1)}, s32[]{:S(2)}) async-start(s8[4718592]{0:T(1024)(128)(4,1)} %bitcast.235), calls=%async_computation.7 | async-start | bytes 8388608
  1007.9 25.3 %copy-start.5 = (f32[768,768]{0,1:T(8,128)S(1)}, f32[768,768]{0,1:T(8,128)}, u32[]{:S(2)}) copy-start(f32[768,768]{0,1:T(8,128)} %broadcast_select_fusion.2) | copy-start | bytes 7077892
Sparse Core Ops, SparseCore 0:
  18.6 53.2 all-gather.1
  251.2 151.3 all-reduce.7
  830.0 63.7 all-reduce.9
  898.1 109.7 all-reduce.11
